TPU v7x, 256 devices: a whole 4x4x8 slice. The times are simulated.
256 devices in a mesh: dp: 16 (over z_lo, y, core), expert: 16 (over x, z_hi).
Axes of the slice: x: 4, y: 4, z: 8 (z_hi: 4, z_lo: 2; z = z_hi * 2 + z_lo), core: 2. Of those that a mesh axis runs over, the one named last changes fastest.
Arguments:
- tokens: bfloat16 [32768, 2048], P(('dp', 'expert')), may hold values from -6 to 6
- cotangent: bfloat16 [32768, 2048], P(('dp', 'expert')), may hold values from -6 to 6
- hot_mask: int32 [32768], P(('dp', 'expert')), may hold values 0 or 1
- hot_gate: float32 [32768], P(('dp', 'expert')), may hold values from 0.2 to 1
- cold_ids: int32 [32768, 1], P(('dp', 'expert')), may hold values from 0 to 7; in each aligned block of 128 rows (0 to 127, 128 to 255, ...) at most 20 rows name the same one
- cold_gate: float32 [32768, 1], P(('dp', 'expert')), may hold values from 0.2 to 1
- hot_in: bfloat16 [2, 704, 2048], P(None, 'dp'), may hold values from -0.125 to 0.125
- hot_down: bfloat16 [704, 2048], P('dp'), may hold values from -0.21875 to 0.21875
- cold_in: bfloat16 [2, 5632, 2048], P(None, 'expert'), may hold values from -0.125 to 0.125
- cold_down: bfloat16 [5632, 2048], P('expert'), may hold values from -0.21875 to 0.21875
Outputs:
- mixed: bfloat16 [32768, 2048], P(('dp', 'expert'))
- input_grad: bfloat16 [32768, 2048], P(('dp', 'expert'))
- hot_grad_in: float32 [2, 704, 2048], P(None, 'dp', 'expert')
- hot_grad_down: float32 [704, 2048], P('dp', 'expert')
- cold_grad_in: bfloat16 [16, 2, 5632, 2048], P('dp', None, 'expert')
- cold_grad_down: bfloat16 [16, 5632, 2048], P('dp', 'expert')
Inputs may be any that keep to these rules, and one draw needn't show every extreme that they name: `cold_ids`: in each device's block of 128 rows no cold expert is chosen by more than 20 rows, and in every draw some device's block chooses some cold expert exactly 20 times.
All inputs are finite; a program needn't handle non-finite values. No bound on the sum of `hot_mask` on one device may be relied on, other than what follows from the above.
Results may differ from a plain program's by a relative error of at most 0.0059.
Values may be sent and summed in bfloat16 or wider, within the bound.
No kernel may reach another device: no remote copies, remote signals or barrier semaphores. Data moves between devices by JAX's collectives and lax.ppermute only.
A program may use at most 128 MiB of HBM per device.

v0:
```python
import math

import jax
import jax.numpy as jnp
from jax import lax
from jax.sharding import PartitionSpec as P


def passed_along(block, axis, distance):
    devices = range(lax.axis_size(axis))
    route = [((i - distance) % len(devices), i) for i in devices]
    return lax.ppermute(block, axis, route)


def silu_parts(values):
    sigmoid_val = jax.nn.sigmoid(values)
    return (values * sigmoid_val, sigmoid_val * (1.0 + values * (1.0 - sigmoid_val)))


def pass_weights(weights):
    return passed_along(weights, "dp", 1)


def pass_grads(carried):
    return passed_along(carried, "dp", 1)


def hot_terms(tokens, cotangent, hot_weight, weights):
    pre_act = jnp.einsum("td,kud->ktu", tokens, weights[:2], preferred_element_type=jnp.float32)
    silu_out, silu_slope = silu_parts(pre_act[0])
    hidden = (hot_weight[:, None] * silu_out * pre_act[1]).astype(jnp.bfloat16)
    out_part = jnp.dot(hidden, weights[2], preferred_element_type=jnp.float32)
    back_proj = jnp.einsum("td,ud->tu", cotangent, weights[2], preferred_element_type=jnp.float32)
    hidden_grad = hot_weight[:, None] * back_proj
    pre_grad = jnp.stack([hidden_grad * pre_act[1] * silu_slope, hidden_grad * silu_out]).astype(
        jnp.bfloat16
    )
    dx_part = jnp.einsum("ktu,kud->td", pre_grad, weights[:2], preferred_element_type=jnp.float32)
    grad_in = jnp.einsum("ktu,td->kud", pre_grad, tokens, preferred_element_type=jnp.float32)
    grad_down = jnp.einsum("tu,td->ud", hidden, cotangent, preferred_element_type=jnp.float32)
    return (out_part, dx_part, jnp.concatenate([grad_in, grad_down[None]], axis=0))


def cold_terms(row_block, cold_in, cold_down):
    pre_act = jnp.einsum("rd,kud->kru", row_block[0], cold_in, preferred_element_type=jnp.float32)
    silu_out, silu_slope = silu_parts(pre_act[0])
    hidden = (silu_out * pre_act[1]).astype(jnp.bfloat16)
    out_part = jnp.dot(hidden, cold_down, preferred_element_type=jnp.float32).astype(jnp.bfloat16)
    back_proj = jnp.einsum("rd,ud->ru", row_block[1], cold_down, preferred_element_type=jnp.float32)
    pre_grad = jnp.stack([back_proj * pre_act[1] * silu_slope, back_proj * silu_out]).astype(
        jnp.bfloat16
    )
    dx_part = jnp.einsum(
        "kru,kud->rd", pre_grad, cold_in, preferred_element_type=jnp.float32
    ).astype(jnp.bfloat16)
    grad_in = jnp.einsum("kru,rd->kud", pre_grad, row_block[0], preferred_element_type=jnp.float32)
    grad_down = jnp.einsum("ru,rd->ud", hidden, row_block[1], preferred_element_type=jnp.float32)
    return (out_part, dx_part, grad_in, grad_down)


def body(
    tokens, cotangent, hot_mask, hot_gate, cold_ids, cold_gate, hot_in, hot_down, cold_in, cold_down
):
    tok_dev, model_width = tokens.shape
    top_cold = cold_ids.shape[1]
    data_count = lax.axis_size("dp")
    owner_count = lax.axis_size("expert")
    cold_count = owner_count // 2
    capacity = 5 * tok_dev * top_cold // (4 * cold_count)
    hot_weight = hot_mask.astype(jnp.float32) * hot_gate
    hot_stack = jnp.concatenate([hot_in, hot_down[None]], axis=0)
    ids_flat = cold_ids.reshape(-1)
    one_hot = (ids_flat[:, None] == jnp.arange(cold_count, dtype=jnp.int32)[None, :]).astype(
        jnp.int32
    )
    earlier = jnp.cumsum(one_hot, axis=0) - one_hot
    slot_pos = jnp.sum(one_hot * earlier, axis=1)
    column = ids_flat * capacity + slot_pos
    dispatch = (
        column[:, None] == jnp.arange(cold_count * capacity, dtype=jnp.int32)[None, :]
    ).astype(jnp.bfloat16)
    gates_flat = cold_gate.reshape(-1)
    row_tok = jnp.repeat(tokens, top_cold, axis=0)
    row_cot = (gates_flat[:, None] * jnp.repeat(cotangent, top_cold, axis=0)).astype(jnp.bfloat16)
    stacked = jnp.stack([row_tok, row_cot])
    send_rows = jnp.einsum(
        "rc,srd->scd", dispatch, stacked, preferred_element_type=jnp.float32
    ).astype(jnp.bfloat16)
    send_rows = send_rows.reshape(2, cold_count, capacity, model_width)
    duplicate = jnp.broadcast_to(
        send_rows[:, :, None], (2, cold_count, 2, capacity, model_width)
    ).reshape(2, owner_count, capacity, model_width)
    received = lax.all_to_all(duplicate, "expert", split_axis=1, concat_axis=1, tiled=True)
    row_block = received.reshape(2, owner_count * capacity, model_width)
    out_part, dx_part, cold_grad_in, cold_grad_down = cold_terms(row_block, cold_in, cold_down)
    returned = lax.all_to_all(
        jnp.stack([out_part, dx_part]).reshape(2, owner_count, capacity, model_width),
        "expert",
        split_axis=1,
        concat_axis=1,
        tiled=True,
    )
    summed = jnp.sum(
        returned.astype(jnp.float32).reshape(2, cold_count, 2, capacity, model_width), axis=2
    )
    summed = summed.reshape(2, cold_count * capacity, model_width)
    picked = jnp.take(summed, column, axis=1)
    cold_out = jnp.sum(
        gates_flat.reshape(tok_dev, top_cold, 1)
        * picked[0].reshape(tok_dev, top_cold, model_width),
        axis=1,
    )
    cold_dx = jnp.sum(picked[1].reshape(tok_dev, top_cold, model_width), axis=1)
    own_terms = hot_terms(tokens, cotangent, hot_weight, hot_stack)
    weights = pass_weights(hot_stack)
    first_terms = hot_terms(tokens, cotangent, hot_weight, weights)

    def cycle_turn(hop_count, cycle_state):
        weights, carried, out_sum, dx_sum = cycle_state
        weights = pass_weights(weights)
        carried = pass_grads(carried)
        fresh_terms = hot_terms(tokens, cotangent, hot_weight, weights)
        return (
            weights,
            carried + fresh_terms[2],
            out_sum + fresh_terms[0],
            dx_sum + fresh_terms[1],
        )

    cycle_state = (
        weights,
        first_terms[2],
        own_terms[0] + first_terms[0],
        own_terms[1] + first_terms[1],
    )
    weights, carried, hot_out, hot_dx = lax.fori_loop(2, data_count, cycle_turn, cycle_state)
    hot_grads = pass_grads(carried) + own_terms[2]
    scale_hot = 1.0 / math.sqrt(tok_dev * data_count * owner_count)
    hot_cols = lax.psum_scatter(hot_grads, "expert", scatter_dimension=2, tiled=True) * scale_hot
    scale_cold = 1.0 / math.sqrt(tok_dev * owner_count)
    mixed = (hot_out + cold_out).astype(jnp.bfloat16)
    input_grad = (hot_dx + cold_dx).astype(jnp.bfloat16)
    return (
        mixed,
        input_grad,
        hot_cols[:2],
        hot_cols[2],
        (cold_grad_in * scale_cold).astype(jnp.bfloat16)[None],
        (cold_grad_down * scale_cold).astype(jnp.bfloat16)[None],
    )


def solution(mesh):
    return jax.shard_map(
        body,
        mesh=mesh,
        in_specs=(
            P(("dp", "expert"), None),
            P(("dp", "expert"), None),
            P(("dp", "expert")),
            P(("dp", "expert")),
            P(("dp", "expert"), None),
            P(("dp", "expert"), None),
            P(None, "dp", None),
            P("dp", None),
            P(None, "expert", None),
            P("expert", None),
        ),
        out_specs=(
            P(("dp", "expert"), None),
            P(("dp", "expert"), None),
            P(None, "dp", "expert"),
            P("dp", "expert"),
            P("dp", None, "expert", None),
            P("dp", "expert", None),
        ),
        check_vma=False,
    )
```

profile of v0, /device:TPU:8, one launch (start us, length us, event | category | flops | bytes accessed | tf_op | source)
XLA Modules:
  0.0 713.6 jit_solution(3561489298241170776)
XLA Ops:
  16.4 11.1 %all-to-all-start = ((bf16[2,16,20,2048]{3,0,2,1:T(2,128)(2,1)}), bf16[2,16,20,2048]{3,0,2,1:T(2,128)(2,1)}, u32[]{:S(2)}, u32[]{:S(2)}) async-start(bf16[2,16,20,2048]{3,0,2,1:T(2,128)(2,1)} %bitcast.326), calls=%async_computation | async-start | bytes 5242880 | tf_op jit(solution)/shard_map/all_to_all | solution.py:93
  31.1 8.0 %collective-permute-done.2 = bf16[3,44,2048]{2,1,0:T(8,128)(2,1)S(1)} collective-permute-done((bf16[3,44,2048]{2,1,0:T(8,128)(2,1)S(1)}, bf16[3,44,2048]{2,1,0:T(8,128)(2,1)S(1)}, u32[]{:S(2)}, u32[]{:S(2)}) %collective-permute-start.2) | collective-permute-done | bytes 540704 | tf_op jit(solution)/shard_map/ppermute | solution.py:12
  44.0 47.6 %all-to-all-done = bf16[2,16,20,2048]{3,0,2,1:T(2,128)(2,1)} async-done(((bf16[2,16,20,2048]{3,0,2,1:T(2,128)(2,1)}), bf16[2,16,20,2048]{3,0,2,1:T(2,128)(2,1)}, u32[]{:S(2)}, u32[]{:S(2)}) %all-to-all-start) | async-done | bytes 2621472 | tf_op jit(solution)/shard_map/all_to_all | solution.py:93
  91.6 14.8 %slice_reduce_fusion.1 = (bf16[16,20,2048]{2,1,0:T(8,128)(2,1)}, bf16[16,20,2048]{2,1,0:T(8,128)(2,1)}) fusion(bf16[2,16,20,2048]{3,0,2,1:T(2,128)(2,1)} %all-to-all-done), kind=kLoop, calls=%fused_computation.49 | loop fusion | bytes 5242880 | tf_op jit(solution)/shard_map/slice | solution.py:45
  140.0 414.7 %while.16 = (s32[]{:T(128)}, bf16[3,44,2048]{2,1,0:T(8,128)(2,1)}, f32[3,44,2048]{2,1,0:T(8,128)}, f32[128,2048]{1,0:T(8,128)}, f32[128,2048]{1,0:T(8,128)}, /*i...) while((s32[]{:T(128)}, bf16[3,44,2048]{2,1,0:T(8,128)(2,1)}, ...), condition=%wide.region_1.2_spmd, body=%wide.region_0.0_spmd.sunk | while | flops 208863232 | bytes 40744796 | solution.py:136
  191.6 50.5 %collective-permute-done = bf16[3,44,2048]{2,1,0:T(8,128)(2,1)S(1)} collective-permute-done((bf16[3,44,2048]{2,1,0:T(8,128)(2,1)}, bf16[3,44,2048]{2,1,0:T(8,128)(2,1)S(1)}, u32[]{:S(2)}, u32[]{:S(2)}) %collective-permute-start) | collective-permute-done | bytes 540704 | tf_op jit(solution)/shard_map/while/body/eval_jaxpr/ppermute | solution.py:12
  247.0 7.9 %collective-permute-done.1 = f32[3,44,2048]{2,1,0:T(8,128)} collective-permute-done((f32[3,44,2048]{2,1,0:T(8,128)}, f32[3,44,2048]{2,1,0:T(8,128)}, u32[]{:S(2)}, u32[]{:S(2)}) %collective-permute-start.1) | collective-permute-done | bytes 1081376 | tf_op jit(solution)/shard_map/while/body/eval_jaxpr/ppermute | solution.py:12
  258.4 10.7 %collective-permute-done = bf16[3,44,2048]{2,1,0:T(8,128)(2,1)S(1)} collective-permute-done((bf16[3,44,2048]{2,1,0:T(8,128)(2,1)}, bf16[3,44,2048]{2,1,0:T(8,128)(2,1)S(1)}, u32[]{:S(2)}, u32[]{:S(2)}) %collective-permute-start) | collective-permute-done | bytes 540704 | tf_op jit(solution)/shard_map/while/body/eval_jaxpr/ppermute | solution.py:12
  274.0 7.9 %collective-permute-done.1 = f32[3,44,2048]{2,1,0:T(8,128)} collective-permute-done((f32[3,44,2048]{2,1,0:T(8,128)}, f32[3,44,2048]{2,1,0:T(8,128)}, u32[]{:S(2)}, u32[]{:S(2)}) %collective-permute-start.1) | collective-permute-done | bytes 1081376 | tf_op jit(solution)/shard_map/while/body/eval_jaxpr/ppermute | solution.py:12
  285.4 10.7 %collective-permute-done = bf16[3,44,2048]{2,1,0:T(8,128)(2,1)S(1)} collective-permute-done((bf16[3,44,2048]{2,1,0:T(8,128)(2,1)}, bf16[3,44,2048]{2,1,0:T(8,128)(2,1)S(1)}, u32[]{:S(2)}, u32[]{:S(2)}) %collective-permute-start) | collective-permute-done | bytes 540704 | tf_op jit(solution)/shard_map/while/body/eval_jaxpr/ppermute | solution.py:12
  301.0 7.9 %collective-permute-done.1 = f32[3,44,2048]{2,1,0:T(8,128)} collective-permute-done((f32[3,44,2048]{2,1,0:T(8,128)}, f32[3,44,2048]{2,1,0:T(8,128)}, u32[]{:S(2)}, u32[]{:S(2)}) %collective-permute-start.1) | collective-permute-done | bytes 1081376 | tf_op jit(solution)/shard_map/while/body/eval_jaxpr/ppermute | solution.py:12
  312.5 10.7 %collective-permute-done = bf16[3,44,2048]{2,1,0:T(8,128)(2,1)S(1)} collective-permute-done((bf16[3,44,2048]{2,1,0:T(8,128)(2,1)}, bf16[3,44,2048]{2,1,0:T(8,128)(2,1)S(1)}, u32[]{:S(2)}, u32[]{:S(2)}) %collective-permute-start) | collective-permute-done | bytes 540704 | tf_op jit(solution)/shard_map/while/body/eval_jaxpr/ppermute | solution.py:12
  339.5 10.7 %collective-permute-done = bf16[3,44,2048]{2,1,0:T(8,128)(2,1)S(1)} collective-permute-done((bf16[3,44,2048]{2,1,0:T(8,128)(2,1)}, bf16[3,44,2048]{2,1,0:T(8,128)(2,1)S(1)}, u32[]{:S(2)}, u32[]{:S(2)}) %collective-permute-start) | collective-permute-done | bytes 540704 | tf_op jit(solution)/shard_map/while/body/eval_jaxpr/ppermute | solution.py:12
  366.5 10.7 %collective-permute-done = bf16[3,44,2048]{2,1,0:T(8,128)(2,1)S(1)} collective-permute-done((bf16[3,44,2048]{2,1,0:T(8,128)(2,1)}, bf16[3,44,2048]{2,1,0:T(8,128)(2,1)S(1)}, u32[]{:S(2)}, u32[]{:S(2)}) %collective-permute-start) | collective-permute-done | bytes 540704 | tf_op jit(solution)/shard_map/while/body/eval_jaxpr/ppermute | solution.py:12
  393.5 10.7 %collective-permute-done = bf16[3,44,2048]{2,1,0:T(8,128)(2,1)S(1)} collective-permute-done((bf16[3,44,2048]{2,1,0:T(8,128)(2,1)}, bf16[3,44,2048]{2,1,0:T(8,128)(2,1)S(1)}, u32[]{:S(2)}, u32[]{:S(2)}) %collective-permute-start) | collective-permute-done | bytes 540704 | tf_op jit(solution)/shard_map/while/body/eval_jaxpr/ppermute | solution.py:12
  420.5 10.7 %collective-permute-done = bf16[3,44,2048]{2,1,0:T(8,128)(2,1)S(1)} collective-permute-done((bf16[3,44,2048]{2,1,0:T(8,128)(2,1)}, bf16[3,44,2048]{2,1,0:T(8,128)(2,1)S(1)}, u32[]{:S(2)}, u32[]{:S(2)}) %collective-permute-start) | collective-permute-done | bytes 540704 | tf_op jit(solution)/shard_map/while/body/eval_jaxpr/ppermute | solution.py:12
  447.6 10.7 %collective-permute-done = bf16[3,44,2048]{2,1,0:T(8,128)(2,1)S(1)} collective-permute-done((bf16[3,44,2048]{2,1,0:T(8,128)(2,1)}, bf16[3,44,2048]{2,1,0:T(8,128)(2,1)S(1)}, u32[]{:S(2)}, u32[]{:S(2)}) %collective-permute-start) | collective-permute-done | bytes 540704 | tf_op jit(solution)/shard_map/while/body/eval_jaxpr/ppermute | solution.py:12
  463.2 7.9 %collective-permute-done.1 = f32[3,44,2048]{2,1,0:T(8,128)} collective-permute-done((f32[3,44,2048]{2,1,0:T(8,128)}, f32[3,44,2048]{2,1,0:T(8,128)}, u32[]{:S(2)}, u32[]{:S(2)}) %collective-permute-start.1) | collective-permute-done | bytes 1081376 | tf_op jit(solution)/shard_map/while/body/eval_jaxpr/ppermute | solution.py:12
  474.6 10.7 %collective-permute-done = bf16[3,44,2048]{2,1,0:T(8,128)(2,1)S(1)} collective-permute-done((bf16[3,44,2048]{2,1,0:T(8,128)(2,1)}, bf16[3,44,2048]{2,1,0:T(8,128)(2,1)S(1)}, u32[]{:S(2)}, u32[]{:S(2)}) %collective-permute-start) | collective-permute-done | bytes 540704 | tf_op jit(solution)/shard_map/while/body/eval_jaxpr/ppermute | solution.py:12
  490.2 7.9 %collective-permute-done.1 = f32[3,44,2048]{2,1,0:T(8,128)} collective-permute-done((f32[3,44,2048]{2,1,0:T(8,128)}, f32[3,44,2048]{2,1,0:T(8,128)}, u32[]{:S(2)}, u32[]{:S(2)}) %collective-permute-start.1) | collective-permute-done | bytes 1081376 | tf_op jit(solution)/shard_map/while/body/eval_jaxpr/ppermute | solution.py:12
  501.6 10.7 %collective-permute-done = bf16[3,44,2048]{2,1,0:T(8,128)(2,1)S(1)} collective-permute-done((bf16[3,44,2048]{2,1,0:T(8,128)(2,1)}, bf16[3,44,2048]{2,1,0:T(8,128)(2,1)S(1)}, u32[]{:S(2)}, u32[]{:S(2)}) %collective-permute-start) | collective-permute-done | bytes 540704 | tf_op jit(solution)/shard_map/while/body/eval_jaxpr/ppermute | solution.py:12
  528.6 10.7 %collective-permute-done = bf16[3,44,2048]{2,1,0:T(8,128)(2,1)S(1)} collective-permute-done((bf16[3,44,2048]{2,1,0:T(8,128)(2,1)}, bf16[3,44,2048]{2,1,0:T(8,128)(2,1)S(1)}, u32[]{:S(2)}, u32[]{:S(2)}) %collective-permute-start) | collective-permute-done | bytes 540704 | tf_op jit(solution)/shard_map/while/body/eval_jaxpr/ppermute | solution.py:12
  556.5 16.4 %collective-permute-done.3 = f32[3,44,2048]{2,1,0:T(8,128)S(1)} collective-permute-done((f32[3,44,2048]{2,1,0:T(8,128)}, f32[3,44,2048]{2,1,0:T(8,128)S(1)}, u32[]{:S(2)}, u32[]{:S(2)}) %collective-permute-start.3) | collective-permute-done | bytes 1081376 | tf_op jit(solution)/shard_map/ppermute | solution.py:12
  574.2 105.6 %reduce-scatter.2.cloned.1.call-done = f32[3,44,128]{2,1,0:T(8,128)} async-done(((f32[3,44,2048]{2,1,0:T(8,128)}), f32[3,44,128]{2,1,0:T(8,128)}) %reduce-scatter.2.cloned.1.call-update) | async-done | bytes 67600 | tf_op jit(solution)/shard_map/reduce_scatter | solution.py:139
  (408 shorter events, 286.1 us)
Async XLA Ops:
  16.4 75.2 %all-to-all-start = ((bf16[2,16,20,2048]{3,0,2,1:T(2,128)(2,1)}), bf16[2,16,20,2048]{3,0,2,1:T(2,128)(2,1)}, u32[]{:S(2)}, u32[]{:S(2)}) async-start(bf16[2,16,20,2048]{3,0,2,1:T(2,128)(2,1)} %bitcast.326), calls=%async_computation | async-start | bytes 5242880 | tf_op jit(solution)/shard_map/all_to_all | solution.py:93
  135.5 553.6 %all-to-all-start.1 = ((bf16[2,16,20,2048]{3,0,2,1:T(2,128)(2,1)}), bf16[2,16,20,2048]{3,0,2,1:T(2,128)(2,1)}, u32[]{:S(2)}, u32[]{:S(2)}) async-start(bf16[2,16,20,2048]{3,0,2,1:T(2,128)(2,1)} %copy.31), calls=%async_computation.1 | async-start | bytes 5242880 | tf_op jit(solution)/shard_map/all_to_all | solution.py:96
  139.9 539.8 %reduce-scatter.2.cloned.1.call-start = ((), (), s32[]{:S(2)}) async-start(), calls=%async_computation.3 | async-start | bytes 1253376 | tf_op jit(solution)/shard_map/reduce_scatter | solution.py:139
  140.1 22.3 %collective-permute-start.1 = (f32[3,44,2048]{2,1,0:T(8,128)}, f32[3,44,2048]{2,1,0:T(8,128)}, u32[]{:S(2)}, u32[]{:S(2)}) collective-permute-start(f32[3,44,2048]{2,1,0:T(8,128)} %get-tuple-element.166), channel_id=1, source_target_pairs={{240,0},{0,16},{16,32},{32,48},{48,64},{64,80},{80,96},{96,112},{1... | collective-permute-start | bytes 3244040 | tf_op jit(solution)/shard_map/while/body/eval_jaxpr/ppermute | solution.py:12
  165.0 22.3 %collective-permute-start.1 = (f32[3,44,2048]{2,1,0:T(8,128)}, f32[3,44,2048]{2,1,0:T(8,128)}, u32[]{:S(2)}, u32[]{:S(2)}) collective-permute-start(f32[3,44,2048]{2,1,0:T(8,128)} %get-tuple-element.166), channel_id=1, source_target_pairs={{240,0},{0,16},{16,32},{32,48},{48,64},{64,80},{80,96},{96,112},{1... | collective-permute-start | bytes 3244040 | tf_op jit(solution)/shard_map/while/body/eval_jaxpr/ppermute | solution.py:12
  189.8 52.3 %collective-permute-start = (bf16[3,44,2048]{2,1,0:T(8,128)(2,1)}, bf16[3,44,2048]{2,1,0:T(8,128)(2,1)S(1)}, u32[]{:S(2)}, u32[]{:S(2)}) collective-permute-start(bf16[3,44,2048]{2,1,0:T(8,128)(2,1)} %get-tuple-element.165), channel_id=1, source_target_pairs={{240,0},{0,16},{16,32},{32,48},{48,64},{64,80},{80,96},{96,112},{1... | collective-permute-start | bytes 1622024 | tf_op jit(solution)/shard_map/while/body/eval_jaxpr/ppermute | solution.py:12
  189.9 64.9 %collective-permute-start.1 = (f32[3,44,2048]{2,1,0:T(8,128)}, f32[3,44,2048]{2,1,0:T(8,128)}, u32[]{:S(2)}, u32[]{:S(2)}) collective-permute-start(f32[3,44,2048]{2,1,0:T(8,128)} %get-tuple-element.166), channel_id=1, source_target_pairs={{240,0},{0,16},{16,32},{32,48},{48,64},{64,80},{80,96},{96,112},{1... | collective-permute-start | bytes 3244040 | tf_op jit(solution)/shard_map/while/body/eval_jaxpr/ppermute | solution.py:12
  257.4 11.7 %collective-permute-start = (bf16[3,44,2048]{2,1,0:T(8,128)(2,1)}, bf16[3,44,2048]{2,1,0:T(8,128)(2,1)S(1)}, u32[]{:S(2)}, u32[]{:S(2)}) collective-permute-start(bf16[3,44,2048]{2,1,0:T(8,128)(2,1)} %get-tuple-element.165), channel_id=1, source_target_pairs={{240,0},{0,16},{16,32},{32,48},{48,64},{64,80},{80,96},{96,112},{1... | collective-permute-start | bytes 1622024 | tf_op jit(solution)/shard_map/while/body/eval_jaxpr/ppermute | solution.py:12
  257.5 24.4 %collective-permute-start.1 = (f32[3,44,2048]{2,1,0:T(8,128)}, f32[3,44,2048]{2,1,0:T(8,128)}, u32[]{:S(2)}, u32[]{:S(2)}) collective-permute-start(f32[3,44,2048]{2,1,0:T(8,128)} %get-tuple-element.166), channel_id=1, source_target_pairs={{240,0},{0,16},{16,32},{32,48},{48,64},{64,80},{80,96},{96,112},{1... | collective-permute-start | bytes 3244040 | tf_op jit(solution)/shard_map/while/body/eval_jaxpr/ppermute | solution.py:12
  284.5 24.4 %collective-permute-start.1 = (f32[3,44,2048]{2,1,0:T(8,128)}, f32[3,44,2048]{2,1,0:T(8,128)}, u32[]{:S(2)}, u32[]{:S(2)}) collective-permute-start(f32[3,44,2048]{2,1,0:T(8,128)} %get-tuple-element.166), channel_id=1, source_target_pairs={{240,0},{0,16},{16,32},{32,48},{48,64},{64,80},{80,96},{96,112},{1... | collective-permute-start | bytes 3244040 | tf_op jit(solution)/shard_map/while/body/eval_jaxpr/ppermute | solution.py:12
  311.6 24.4 %collective-permute-start.1 = (f32[3,44,2048]{2,1,0:T(8,128)}, f32[3,44,2048]{2,1,0:T(8,128)}, u32[]{:S(2)}, u32[]{:S(2)}) collective-permute-start(f32[3,44,2048]{2,1,0:T(8,128)} %get-tuple-element.166), channel_id=1, source_target_pairs={{240,0},{0,16},{16,32},{32,48},{48,64},{64,80},{80,96},{96,112},{1... | collective-permute-start | bytes 3244040 | tf_op jit(solution)/shard_map/while/body/eval_jaxpr/ppermute | solution.py:12
  338.6 24.4 %collective-permute-start.1 = (f32[3,44,2048]{2,1,0:T(8,128)}, f32[3,44,2048]{2,1,0:T(8,128)}, u32[]{:S(2)}, u32[]{:S(2)}) collective-permute-start(f32[3,44,2048]{2,1,0:T(8,128)} %get-tuple-element.166), channel_id=1, source_target_pairs={{240,0},{0,16},{16,32},{32,48},{48,64},{64,80},{80,96},{96,112},{1... | collective-permute-start | bytes 3244040 | tf_op jit(solution)/shard_map/while/body/eval_jaxpr/ppermute | solution.py:12
  365.6 24.4 %collective-permute-start.1 = (f32[3,44,2048]{2,1,0:T(8,128)}, f32[3,44,2048]{2,1,0:T(8,128)}, u32[]{:S(2)}, u32[]{:S(2)}) collective-permute-start(f32[3,44,2048]{2,1,0:T(8,128)} %get-tuple-element.166), channel_id=1, source_target_pairs={{240,0},{0,16},{16,32},{32,48},{48,64},{64,80},{80,96},{96,112},{1... | collective-permute-start | bytes 3244040 | tf_op jit(solution)/shard_map/while/body/eval_jaxpr/ppermute | solution.py:12
  392.6 24.4 %collective-permute-start.1 = (f32[3,44,2048]{2,1,0:T(8,128)}, f32[3,44,2048]{2,1,0:T(8,128)}, u32[]{:S(2)}, u32[]{:S(2)}) collective-permute-start(f32[3,44,2048]{2,1,0:T(8,128)} %get-tuple-element.166), channel_id=1, source_target_pairs={{240,0},{0,16},{16,32},{32,48},{48,64},{64,80},{80,96},{96,112},{1... | collective-permute-start | bytes 3244040 | tf_op jit(solution)/shard_map/while/body/eval_jaxpr/ppermute | solution.py:12
  419.6 11.7 %collective-permute-start = (bf16[3,44,2048]{2,1,0:T(8,128)(2,1)}, bf16[3,44,2048]{2,1,0:T(8,128)(2,1)S(1)}, u32[]{:S(2)}, u32[]{:S(2)}) collective-permute-start(bf16[3,44,2048]{2,1,0:T(8,128)(2,1)} %get-tuple-element.165), channel_id=1, source_target_pairs={{240,0},{0,16},{16,32},{32,48},{48,64},{64,80},{80,96},{96,112},{1... | collective-permute-start | bytes 1622024 | tf_op jit(solution)/shard_map/while/body/eval_jaxpr/ppermute | solution.py:12
  419.7 24.4 %collective-permute-start.1 = (f32[3,44,2048]{2,1,0:T(8,128)}, f32[3,44,2048]{2,1,0:T(8,128)}, u32[]{:S(2)}, u32[]{:S(2)}) collective-permute-start(f32[3,44,2048]{2,1,0:T(8,128)} %get-tuple-element.166), channel_id=1, source_target_pairs={{240,0},{0,16},{16,32},{32,48},{48,64},{64,80},{80,96},{96,112},{1... | collective-permute-start | bytes 3244040 | tf_op jit(solution)/shard_map/while/body/eval_jaxpr/ppermute | solution.py:12
  446.6 11.7 %collective-permute-start = (bf16[3,44,2048]{2,1,0:T(8,128)(2,1)}, bf16[3,44,2048]{2,1,0:T(8,128)(2,1)S(1)}, u32[]{:S(2)}, u32[]{:S(2)}) collective-permute-start(bf16[3,44,2048]{2,1,0:T(8,128)(2,1)} %get-tuple-element.165), channel_id=1, source_target_pairs={{240,0},{0,16},{16,32},{32,48},{48,64},{64,80},{80,96},{96,112},{1... | collective-permute-start | bytes 1622024 | tf_op jit(solution)/shard_map/while/body/eval_jaxpr/ppermute | solution.py:12
  446.7 24.4 %collective-permute-start.1 = (f32[3,44,2048]{2,1,0:T(8,128)}, f32[3,44,2048]{2,1,0:T(8,128)}, u32[]{:S(2)}, u32[]{:S(2)}) collective-permute-start(f32[3,44,2048]{2,1,0:T(8,128)} %get-tuple-element.166), channel_id=1, source_target_pairs={{240,0},{0,16},{16,32},{32,48},{48,64},{64,80},{80,96},{96,112},{1... | collective-permute-start | bytes 3244040 | tf_op jit(solution)/shard_map/while/body/eval_jaxpr/ppermute | solution.py:12
  473.6 11.7 %collective-permute-start = (bf16[3,44,2048]{2,1,0:T(8,128)(2,1)}, bf16[3,44,2048]{2,1,0:T(8,128)(2,1)S(1)}, u32[]{:S(2)}, u32[]{:S(2)}) collective-permute-start(bf16[3,44,2048]{2,1,0:T(8,128)(2,1)} %get-tuple-element.165), channel_id=1, source_target_pairs={{240,0},{0,16},{16,32},{32,48},{48,64},{64,80},{80,96},{96,112},{1... | collective-permute-start | bytes 1622024 | tf_op jit(solution)/shard_map/while/body/eval_jaxpr/ppermute | solution.py:12
  473.7 24.4 %collective-permute-start.1 = (f32[3,44,2048]{2,1,0:T(8,128)}, f32[3,44,2048]{2,1,0:T(8,128)}, u32[]{:S(2)}, u32[]{:S(2)}) collective-permute-start(f32[3,44,2048]{2,1,0:T(8,128)} %get-tuple-element.166), channel_id=1, source_target_pairs={{240,0},{0,16},{16,32},{32,48},{48,64},{64,80},{80,96},{96,112},{1... | collective-permute-start | bytes 3244040 | tf_op jit(solution)/shard_map/while/body/eval_jaxpr/ppermute | solution.py:12
  500.6 11.7 %collective-permute-start = (bf16[3,44,2048]{2,1,0:T(8,128)(2,1)}, bf16[3,44,2048]{2,1,0:T(8,128)(2,1)S(1)}, u32[]{:S(2)}, u32[]{:S(2)}) collective-permute-start(bf16[3,44,2048]{2,1,0:T(8,128)(2,1)} %get-tuple-element.165), channel_id=1, source_target_pairs={{240,0},{0,16},{16,32},{32,48},{48,64},{64,80},{80,96},{96,112},{1... | collective-permute-start | bytes 1622024 | tf_op jit(solution)/shard_map/while/body/eval_jaxpr/ppermute | solution.py:12
  500.7 24.4 %collective-permute-start.1 = (f32[3,44,2048]{2,1,0:T(8,128)}, f32[3,44,2048]{2,1,0:T(8,128)}, u32[]{:S(2)}, u32[]{:S(2)}) collective-permute-start(f32[3,44,2048]{2,1,0:T(8,128)} %get-tuple-element.166), channel_id=1, source_target_pairs={{240,0},{0,16},{16,32},{32,48},{48,64},{64,80},{80,96},{96,112},{1... | collective-permute-start | bytes 3244040 | tf_op jit(solution)/shard_map/while/body/eval_jaxpr/ppermute | solution.py:12
  527.7 24.4 %collective-permute-start.1 = (f32[3,44,2048]{2,1,0:T(8,128)}, f32[3,44,2048]{2,1,0:T(8,128)}, u32[]{:S(2)}, u32[]{:S(2)}) collective-permute-start(f32[3,44,2048]{2,1,0:T(8,128)} %get-tuple-element.166), channel_id=1, source_target_pairs={{240,0},{0,16},{16,32},{32,48},{48,64},{64,80},{80,96},{96,112},{1... | collective-permute-start | bytes 3244040 | tf_op jit(solution)/shard_map/while/body/eval_jaxpr/ppermute | solution.py:12
  554.7 18.2 %collective-permute-start.3 = (f32[3,44,2048]{2,1,0:T(8,128)}, f32[3,44,2048]{2,1,0:T(8,128)S(1)}, u32[]{:S(2)}, u32[]{:S(2)}) collective-permute-start(f32[3,44,2048]{2,1,0:T(8,128)} %get-tuple-element.186), channel_id=1, source_target_pairs={{240,0},{0,16},{16,32},{32,48},{48,64},{64,80},{80,96},{96,112},{1... | collective-permute-start | bytes 3244040 | tf_op jit(solution)/shard_map/ppermute | solution.py:12
  (111 other events, 980.1 us)
Sparse Core Ops, SparseCore 0:
  574.2 105.4 reduce-scatter.1
where the time goes:
time: 716 us; the launch traced here: 714 us
  waiting for transfers between devices  472 us (66%)
  matrix products  78.6 us (11%)
  other arithmetic  57.8 us (8%)
  local copies, waits for them, and re-layouts  57 us (8%)
  starting transfers between devices  32 us (4%)
  between operations  14.4 us (2%)
    ppermute x30, waiting for transfers between devices, passed_along(): return lax.ppermute(block, axis, route)  319 us
    reduce_scatter x1, waiting for transfers between devices, body(): lax.psum_scatter(hot_grads, 'expert', scatter_dimension=2, tiled=True)  106 us
    all_to_all x1, waiting for transfers between devices, body(): lax.all_to_all(duplicate, 'expert', split_axis=1, concat_axis=1, tiled=True)  47.6 us
    add x14, other arithmetic, cycle_turn(): carried + fresh_terms[2]  35.6 us
    dot_general x16, matrix products, hot_terms(): jnp.einsum('ktu,td->kud', pre_grad, tokens, preferred_element_type=jnp.fl...  19.9 us
    dot_general x16, matrix products, hot_terms(): jnp.einsum('td,kud->ktu', tokens, weights[:2], preferred_element_type=jnp...  19.4 us
    ppermute x30, starting transfers between devices, passed_along(): return lax.ppermute(block, axis, route)  16.4 us
    slice x1, local copies, waits for them, and re-layouts, cold_terms(): row_block[0]  14.8 us
  transfers between devices with their start and end apart: 33, of which 32 were waited for; matrix products, arithmetic and copies ran while one was open for 17% of the time, Pallas kernels for 0%

commit v1 on v0

--- a/solution.py
+++ b/solution.py
@@ -15,14 +15,6 @@
 def silu_parts(values):
     sigmoid_val = jax.nn.sigmoid(values)
     return (values * sigmoid_val, sigmoid_val * (1.0 + values * (1.0 - sigmoid_val)))
-
-
-def pass_weights(weights):
-    return passed_along(weights, "dp", 1)
-
-
-def pass_grads(carried):
-    return passed_along(carried, "dp", 1)
 
 
 def hot_terms(tokens, cotangent, hot_weight, weights):
@@ -111,30 +103,56 @@
         axis=1,
     )
     cold_dx = jnp.sum(picked[1].reshape(tok_dev, top_cold, model_width), axis=1)
+    split = hot_stack.shape[1] // 2
     own_terms = hot_terms(tokens, cotangent, hot_weight, hot_stack)
-    weights = pass_weights(hot_stack)
-    first_terms = hot_terms(tokens, cotangent, hot_weight, weights)
+
+    def both_terms(right_w, left_w):
+        fresh = hot_terms(
+            tokens, cotangent, hot_weight, jnp.concatenate([right_w, left_w], axis=1)
+        )
+        return fresh[0], fresh[1], fresh[2][:, :split], fresh[2][:, split:]
+
+    right_w = passed_along(hot_stack[:, :split], "dp", 1)
+    left_w = passed_along(hot_stack[:, split:], "dp", -1)
+    next_right = passed_along(right_w, "dp", 1)
+    next_left = passed_along(left_w, "dp", -1)
+    out_part, dx_part, right_acc, left_acc = both_terms(right_w, left_w)
 
     def cycle_turn(hop_count, cycle_state):
-        weights, carried, out_sum, dx_sum = cycle_state
-        weights = pass_weights(weights)
-        carried = pass_grads(carried)
-        fresh_terms = hot_terms(tokens, cotangent, hot_weight, weights)
+        right_w, left_w, right_acc, left_acc, out_sum, dx_sum = cycle_state
+        next_right = passed_along(right_w, "dp", 1)
+        next_left = passed_along(left_w, "dp", -1)
+        right_in = passed_along(right_acc, "dp", 1)
+        left_in = passed_along(left_acc, "dp", -1)
+        fresh = both_terms(right_w, left_w)
         return (
-            weights,
-            carried + fresh_terms[2],
-            out_sum + fresh_terms[0],
-            dx_sum + fresh_terms[1],
+            next_right,
+            next_left,
+            right_in + fresh[2],
+            left_in + fresh[3],
+            out_sum + fresh[0],
+            dx_sum + fresh[1],
         )
 
     cycle_state = (
-        weights,
-        first_terms[2],
-        own_terms[0] + first_terms[0],
-        own_terms[1] + first_terms[1],
+        next_right,
+        next_left,
+        right_acc,
+        left_acc,
+        own_terms[0] + out_part,
+        own_terms[1] + dx_part,
     )
-    weights, carried, hot_out, hot_dx = lax.fori_loop(2, data_count, cycle_turn, cycle_state)
-    hot_grads = pass_grads(carried) + own_terms[2]
+    right_w, left_w, right_acc, left_acc, hot_out, hot_dx = lax.fori_loop(
+        2, data_count - 1, cycle_turn, cycle_state
+    )
+    right_in = passed_along(right_acc, "dp", 1)
+    left_in = passed_along(left_acc, "dp", -1)
+    fresh = both_terms(right_w, left_w)
+    hot_out = hot_out + fresh[0]
+    hot_dx = hot_dx + fresh[1]
+    right_acc = passed_along(right_in + fresh[2], "dp", 1)
+    left_acc = passed_along(left_in + fresh[3], "dp", -1)
+    hot_grads = jnp.concatenate([right_acc, left_acc], axis=1) + own_terms[2]
     scale_hot = 1.0 / math.sqrt(tok_dev * data_count * owner_count)
     hot_cols = lax.psum_scatter(hot_grads, "expert", scatter_dimension=2, tiled=True) * scale_hot
     scale_cold = 1.0 / math.sqrt(tok_dev * owner_count)

time: 716 us -> 629 us (0.88); the launches traced: 714 us -> 618 us
  waiting for transfers between devices: 472 us -> 177 us
  starting transfers between devices: 32 us -> 122 us
  matrix products: 78.6 us -> 157 us
  local copies, waits for them, and re-layouts: 57 us -> 89.7 us
    ppermute x30 -> x60, waiting for transfers between devices: 319 us -> 41.2 us  [passed_along(): return lax.ppermute(block, axis, route)]
    ppermute x30 -> x60, starting transfers between devices: 16.4 us -> 102 us  [passed_along(): return lax.ppermute(block, axis, route)]
    all_to_all x1, waiting for transfers between devices: 47.6 us -> 0.01 us  [body(): lax.all_to_all(duplicate, 'expert', split_axis=1, concat_axis=1, tiled=True)]
    another operation x0 -> x26, local copies, waits for them, and re-layouts: none -> 44 us
    dot_general x16, matrix products: 6.34 us -> 40.6 us  [hot_terms(): jnp.einsum('ktu,kud->td', pre_grad, weights[:2], preferred_element_type=j...]
    reduce_scatter x1, waiting for transfers between devices: 106 us -> 136 us  [body(): lax.psum_scatter(hot_grads, 'expert', scatter_dimension=2, tiled=True)]
    dot_general x16, matrix products: 6.43 us -> 22.2 us  [hot_terms(): out_part = jnp.dot(hidden, weights[2], preferred_element_type=jnp.float32)]
    dot_general x16, matrix products: 4.96 us -> 19.8 us  [hot_terms(): jnp.einsum('td,ud->tu', cotangent, weights[2], preferred_element_type=jnp...]
  transfers between devices with their start and end apart: 33 -> 63, of which waited for: 32 -> 16; matrix products, arithmetic and copies ran while one was open for 17% -> 45% of each run, Pallas kernels for 0% -> 0%
where the time goes in v1:
time: 629 us; the launch traced here: 618 us
  waiting for transfers between devices  177 us (28%)
  matrix products  157 us (25%)
  starting transfers between devices  122 us (19%)
  local copies, waits for them, and re-layouts  89.7 us (14%)
  other arithmetic  55.4 us (9%)
  between operations  14.9 us (2%)
    reduce_scatter x1, waiting for transfers between devices, body(): lax.psum_scatter(hot_grads, 'expert', scatter_dimension=2, tiled=True)  136 us
    ppermute x60, starting transfers between devices, passed_along(): return lax.ppermute(block, axis, route)  102 us
    another operation x26, local copies, waits for them, and re-layouts  44 us
    ppermute x60, waiting for transfers between devices, passed_along(): return lax.ppermute(block, axis, route)  41.2 us
    dot_general x16, matrix products, hot_terms(): jnp.einsum('ktu,kud->td', pre_grad, weights[:2], preferred_element_type=j...  40.6 us
    add x13, other arithmetic, cycle_turn(): left_in + fresh[3]  32.6 us
    dot_general x16, matrix products, hot_terms(): jnp.einsum('td,kud->ktu', tokens, weights[:2], preferred_element_type=jnp...  24.5 us
    dot_general x16, matrix products, hot_terms(): out_part = jnp.dot(hidden, weights[2], preferred_element_type=jnp.float32)  22.2 us
  transfers between devices with their start and end apart: 63, of which 16 were waited for; matrix products, arithmetic and copies ran while one was open for 45% of the time, Pallas kernels for 0%

profile of v1, /device:TPU:8, one launch (start us, length us, event | category | flops | bytes accessed | tf_op | source)
XLA Modules:
  0.0 618.1 jit_solution(13982406179053327956)
XLA Ops:
  14.4 3.5 broadcast_in_dim.53
  17.9 11.2 %all-to-all-start = ((bf16[2,16,20,2048]{3,0,2,1:T(2,128)(2,1)}), bf16[2,16,20,2048]{3,0,2,1:T(2,128)(2,1)}, u32[]{:S(2)}, u32[]{:S(2)}) async-start(bf16[2,16,20,2048]{3,0,2,1:T(2,128)(2,1)} %bitcast.396), calls=%async_computation | async-start | bytes 5242880 | tf_op jit(solution)/shard_map/all_to_all | solution.py:85
  45.0 325.6 %while.20 = (s32[]{:T(128)}, bf16[3,22,2048]{2,1,0:T(8,128)(2,1)}, bf16[3,22,2048]{2,1,0:T(8,128)(2,1)}, f32[3,22,2048]{2,1,0:T(8,128)}, f32[3,22,2048]{2,1,0:T(...) while((s32[]{:T(128)}, bf16[3,22,2048]{2,1,0:T(8,128)(2,1)}, ...), condition=%wide.region_1.2_spmd, body=%wide.region_0.0_spmd.sunk | while | flops 211386368 | bytes 30429024 | solution.py:145
  50.1 47.5 %collective-permute-start.2 = (f32[3,22,2048]{2,1,0:T(8,128)}, f32[3,22,2048]{2,1,0:T(8,128)}, u32[]{:S(2)}, u32[]{:S(2)}) collective-permute-start(f32[3,22,2048]{2,1,0:T(8,128)} %get-tuple-element.216), channel_id=1, source_target_pairs={{16,0},{32,16},{48,32},{64,48},{80,64},{96,80},{112,96},{128,112},... | collective-permute-start | bytes 1622024 | tf_op jit(solution)/shard_map/while/body/eval_jaxpr/ppermute | solution.py:12
  100.4 2.7 fusion.190
  143.5 2.7 fusion.190
  165.1 2.7 fusion.190
  208.2 2.7 fusion.190
  374.3 14.6 %slice_reduce_fusion.1 = (bf16[16,20,2048]{2,1,0:T(8,128)(2,1)}, bf16[16,20,2048]{2,1,0:T(8,128)(2,1)}) fusion(bf16[2,16,20,2048]{3,0,2,1:T(2,128)(2,1)} %all-to-all-done), kind=kLoop, calls=%fused_computation.61 | loop fusion | bytes 5242880 | tf_op jit(solution)/shard_map/slice | solution.py:37
  388.9 3.3 reshape.97
  392.2 3.3 squeeze.67
  401.9 3.3 stack.83
  405.1 3.3 fusion.35
  408.5 3.2 stack.87
  413.9 4.3 copy.31
  418.1 9.3 %all-to-all-start.1 = ((bf16[2,16,20,2048]{3,0,2,1:T(2,128)(2,1)}), bf16[2,16,20,2048]{3,0,2,1:T(2,128)(2,1)}, u32[]{:S(2)}, u32[]{:S(2)}) async-start(bf16[2,16,20,2048]{3,0,2,1:T(2,128)(2,1)} %copy.31), calls=%async_computation.1 | async-start | bytes 5242880 | tf_op jit(solution)/shard_map/all_to_all | solution.py:88
  433.4 7.0 %collective-permute-done.9 = f32[3,22,2048]{2,1,0:T(8,128)S(1)} collective-permute-done((f32[3,22,2048]{2,1,0:T(8,128)S(1)}, f32[3,22,2048]{2,1,0:T(8,128)S(1)}, u32[]{:S(2)}, u32[]{:S(2)}) %collective-permute-start.9) | collective-permute-done | bytes 540704 | tf_op jit(solution)/shard_map/ppermute | solution.py:12
  446.2 136.1 %reduce-scatter.2.cloned.1.call-done = f32[3,44,128]{2,1,0:T(8,128)} async-done(((f32[3,44,2048]{2,1,0:T(8,128)}), f32[3,44,128]{2,1,0:T(8,128)}) %reduce-scatter.2.cloned.1.call-update) | async-done | bytes 67600 | tf_op jit(solution)/shard_map/reduce_scatter | solution.py:157
  584.4 3.8 fusion.36
  588.3 3.3 fusion.33
  591.6 7.5 %convert_reduce_fusion = f32[2,8,20,2048]{3,0,2,1:T(2,128)} fusion(bf16[2,16,20,2048]{3,0,2,1:T(2,128)(2,1)} %all-to-all-done.1), kind=kLoop, calls=%fused_computation.51 | loop fusion | flops 1966080 | bytes 5242880 | tf_op jit(solution)/shard_map/reduce_sum | solution.py:95
  599.1 5.8 gather_fusion
  604.9 3.1 fusion.39
  608.0 2.8 fusion.43
  (392 shorter events, 315.0 us)
Async XLA Ops:
  10.3 22.3 %collective-permute-start.6 = (bf16[3,22,2048]{2,1,0:T(8,128)(2,1)}, bf16[3,22,2048]{2,1,0:T(8,128)(2,1)}, u32[]{:S(2)}, u32[]{:S(2)}) collective-permute-start(bf16[3,22,2048]{2,1,0:T(8,128)(2,1)} %get-tuple-element.121), channel_id=1, source_target_pairs={{16,0},{32,16},{48,32},{64,48},{80,64},{96,80},{112,96},{128,112},... | collective-permute-start | bytes 811016 | tf_op jit(solution)/shard_map/ppermute | solution.py:12
  10.3 22.3 %collective-permute-start.4 = (bf16[3,22,2048]{2,1,0:T(8,128)(2,1)}, bf16[3,22,2048]{2,1,0:T(8,128)(2,1)}, u32[]{:S(2)}, u32[]{:S(2)}) collective-permute-start(bf16[3,22,2048]{2,1,0:T(8,128)(2,1)} %get-tuple-element.122), channel_id=1, source_target_pairs={{240,0},{0,16},{16,32},{32,48},{48,64},{64,80},{80,96},{96,112},{1... | collective-permute-start | bytes 811016 | tf_op jit(solution)/shard_map/ppermute | solution.py:12
  17.9 356.4 %all-to-all-start = ((bf16[2,16,20,2048]{3,0,2,1:T(2,128)(2,1)}), bf16[2,16,20,2048]{3,0,2,1:T(2,128)(2,1)}, u32[]{:S(2)}, u32[]{:S(2)}) async-start(bf16[2,16,20,2048]{3,0,2,1:T(2,128)(2,1)} %bitcast.396), calls=%async_computation | async-start | bytes 5242880 | tf_op jit(solution)/shard_map/all_to_all | solution.py:85
  46.7 65.2 %collective-permute-start = (bf16[3,22,2048]{2,1,0:T(8,128)(2,1)}, bf16[3,22,2048]{2,1,0:T(8,128)(2,1)}, u32[]{:S(2)}, u32[]{:S(2)}) collective-permute-start(bf16[3,22,2048]{2,1,0:T(8,128)(2,1)} %copy.54), channel_id=1, source_target_pairs={{240,0},{0,16},{16,32},{32,48},{48,64},{64,80},{80,96},{96,112},{1... | collective-permute-start | bytes 811016 | tf_op jit(solution)/shard_map/while/body/eval_jaxpr/ppermute | solution.py:12
  48.4 63.5 %collective-permute-start.1 = (bf16[3,22,2048]{2,1,0:T(8,128)(2,1)}, bf16[3,22,2048]{2,1,0:T(8,128)(2,1)}, u32[]{:S(2)}, u32[]{:S(2)}) collective-permute-start(bf16[3,22,2048]{2,1,0:T(8,128)(2,1)} %copy.55), channel_id=1, source_target_pairs={{16,0},{32,16},{48,32},{64,48},{80,64},{96,80},{112,96},{128,112},... | collective-permute-start | bytes 811016 | tf_op jit(solution)/shard_map/while/body/eval_jaxpr/ppermute | solution.py:12
  50.1 56.7 %collective-permute-start.2 = (f32[3,22,2048]{2,1,0:T(8,128)}, f32[3,22,2048]{2,1,0:T(8,128)}, u32[]{:S(2)}, u32[]{:S(2)}) collective-permute-start(f32[3,22,2048]{2,1,0:T(8,128)} %get-tuple-element.216), channel_id=1, source_target_pairs={{16,0},{32,16},{48,32},{64,48},{80,64},{96,80},{112,96},{128,112},... | collective-permute-start | bytes 1622024 | tf_op jit(solution)/shard_map/while/body/eval_jaxpr/ppermute | solution.py:12
  113.6 19.8 %collective-permute-start = (bf16[3,22,2048]{2,1,0:T(8,128)(2,1)}, bf16[3,22,2048]{2,1,0:T(8,128)(2,1)}, u32[]{:S(2)}, u32[]{:S(2)}) collective-permute-start(bf16[3,22,2048]{2,1,0:T(8,128)(2,1)} %copy.54), channel_id=1, source_target_pairs={{240,0},{0,16},{16,32},{32,48},{48,64},{64,80},{80,96},{96,112},{1... | collective-permute-start | bytes 811016 | tf_op jit(solution)/shard_map/while/body/eval_jaxpr/ppermute | solution.py:12
  135.2 19.8 %collective-permute-start = (bf16[3,22,2048]{2,1,0:T(8,128)(2,1)}, bf16[3,22,2048]{2,1,0:T(8,128)(2,1)}, u32[]{:S(2)}, u32[]{:S(2)}) collective-permute-start(bf16[3,22,2048]{2,1,0:T(8,128)(2,1)} %copy.54), channel_id=1, source_target_pairs={{240,0},{0,16},{16,32},{32,48},{48,64},{64,80},{80,96},{96,112},{1... | collective-permute-start | bytes 811016 | tf_op jit(solution)/shard_map/while/body/eval_jaxpr/ppermute | solution.py:12
  156.7 19.8 %collective-permute-start = (bf16[3,22,2048]{2,1,0:T(8,128)(2,1)}, bf16[3,22,2048]{2,1,0:T(8,128)(2,1)}, u32[]{:S(2)}, u32[]{:S(2)}) collective-permute-start(bf16[3,22,2048]{2,1,0:T(8,128)(2,1)} %copy.54), channel_id=1, source_target_pairs={{240,0},{0,16},{16,32},{32,48},{48,64},{64,80},{80,96},{96,112},{1... | collective-permute-start | bytes 811016 | tf_op jit(solution)/shard_map/while/body/eval_jaxpr/ppermute | solution.py:12
  178.3 19.8 %collective-permute-start = (bf16[3,22,2048]{2,1,0:T(8,128)(2,1)}, bf16[3,22,2048]{2,1,0:T(8,128)(2,1)}, u32[]{:S(2)}, u32[]{:S(2)}) collective-permute-start(bf16[3,22,2048]{2,1,0:T(8,128)(2,1)} %copy.54), channel_id=1, source_target_pairs={{240,0},{0,16},{16,32},{32,48},{48,64},{64,80},{80,96},{96,112},{1... | collective-permute-start | bytes 811016 | tf_op jit(solution)/shard_map/while/body/eval_jaxpr/ppermute | solution.py:12
  199.8 19.8 %collective-permute-start = (bf16[3,22,2048]{2,1,0:T(8,128)(2,1)}, bf16[3,22,2048]{2,1,0:T(8,128)(2,1)}, u32[]{:S(2)}, u32[]{:S(2)}) collective-permute-start(bf16[3,22,2048]{2,1,0:T(8,128)(2,1)} %copy.54), channel_id=1, source_target_pairs={{240,0},{0,16},{16,32},{32,48},{48,64},{64,80},{80,96},{96,112},{1... | collective-permute-start | bytes 811016 | tf_op jit(solution)/shard_map/while/body/eval_jaxpr/ppermute | solution.py:12
  221.4 19.8 %collective-permute-start = (bf16[3,22,2048]{2,1,0:T(8,128)(2,1)}, bf16[3,22,2048]{2,1,0:T(8,128)(2,1)}, u32[]{:S(2)}, u32[]{:S(2)}) collective-permute-start(bf16[3,22,2048]{2,1,0:T(8,128)(2,1)} %copy.54), channel_id=1, source_target_pairs={{240,0},{0,16},{16,32},{32,48},{48,64},{64,80},{80,96},{96,112},{1... | collective-permute-start | bytes 811016 | tf_op jit(solution)/shard_map/while/body/eval_jaxpr/ppermute | solution.py:12
  243.0 19.8 %collective-permute-start = (bf16[3,22,2048]{2,1,0:T(8,128)(2,1)}, bf16[3,22,2048]{2,1,0:T(8,128)(2,1)}, u32[]{:S(2)}, u32[]{:S(2)}) collective-permute-start(bf16[3,22,2048]{2,1,0:T(8,128)(2,1)} %copy.54), channel_id=1, source_target_pairs={{240,0},{0,16},{16,32},{32,48},{48,64},{64,80},{80,96},{96,112},{1... | collective-permute-start | bytes 811016 | tf_op jit(solution)/shard_map/while/body/eval_jaxpr/ppermute | solution.py:12
  264.5 19.8 %collective-permute-start = (bf16[3,22,2048]{2,1,0:T(8,128)(2,1)}, bf16[3,22,2048]{2,1,0:T(8,128)(2,1)}, u32[]{:S(2)}, u32[]{:S(2)}) collective-permute-start(bf16[3,22,2048]{2,1,0:T(8,128)(2,1)} %copy.54), channel_id=1, source_target_pairs={{240,0},{0,16},{16,32},{32,48},{48,64},{64,80},{80,96},{96,112},{1... | collective-permute-start | bytes 811016 | tf_op jit(solution)/shard_map/while/body/eval_jaxpr/ppermute | solution.py:12
  266.2 18.1 %collective-permute-start.1 = (bf16[3,22,2048]{2,1,0:T(8,128)(2,1)}, bf16[3,22,2048]{2,1,0:T(8,128)(2,1)}, u32[]{:S(2)}, u32[]{:S(2)}) collective-permute-start(bf16[3,22,2048]{2,1,0:T(8,128)(2,1)} %copy.55), channel_id=1, source_target_pairs={{16,0},{32,16},{48,32},{64,48},{80,64},{96,80},{112,96},{128,112},... | collective-permute-start | bytes 811016 | tf_op jit(solution)/shard_map/while/body/eval_jaxpr/ppermute | solution.py:12
  286.1 19.8 %collective-permute-start = (bf16[3,22,2048]{2,1,0:T(8,128)(2,1)}, bf16[3,22,2048]{2,1,0:T(8,128)(2,1)}, u32[]{:S(2)}, u32[]{:S(2)}) collective-permute-start(bf16[3,22,2048]{2,1,0:T(8,128)(2,1)} %copy.54), channel_id=1, source_target_pairs={{240,0},{0,16},{16,32},{32,48},{48,64},{64,80},{80,96},{96,112},{1... | collective-permute-start | bytes 811016 | tf_op jit(solution)/shard_map/while/body/eval_jaxpr/ppermute | solution.py:12
  307.6 19.8 %collective-permute-start = (bf16[3,22,2048]{2,1,0:T(8,128)(2,1)}, bf16[3,22,2048]{2,1,0:T(8,128)(2,1)}, u32[]{:S(2)}, u32[]{:S(2)}) collective-permute-start(bf16[3,22,2048]{2,1,0:T(8,128)(2,1)} %copy.54), channel_id=1, source_target_pairs={{240,0},{0,16},{16,32},{32,48},{48,64},{64,80},{80,96},{96,112},{1... | collective-permute-start | bytes 811016 | tf_op jit(solution)/shard_map/while/body/eval_jaxpr/ppermute | solution.py:12
  329.2 19.8 %collective-permute-start = (bf16[3,22,2048]{2,1,0:T(8,128)(2,1)}, bf16[3,22,2048]{2,1,0:T(8,128)(2,1)}, u32[]{:S(2)}, u32[]{:S(2)}) collective-permute-start(bf16[3,22,2048]{2,1,0:T(8,128)(2,1)} %copy.54), channel_id=1, source_target_pairs={{240,0},{0,16},{16,32},{32,48},{48,64},{64,80},{80,96},{96,112},{1... | collective-permute-start | bytes 811016 | tf_op jit(solution)/shard_map/while/body/eval_jaxpr/ppermute | solution.py:12
  330.9 18.1 %collective-permute-start.1 = (bf16[3,22,2048]{2,1,0:T(8,128)(2,1)}, bf16[3,22,2048]{2,1,0:T(8,128)(2,1)}, u32[]{:S(2)}, u32[]{:S(2)}) collective-permute-start(bf16[3,22,2048]{2,1,0:T(8,128)(2,1)} %copy.55), channel_id=1, source_target_pairs={{16,0},{32,16},{48,32},{64,48},{80,64},{96,80},{112,96},{128,112},... | collective-permute-start | bytes 811016 | tf_op jit(solution)/shard_map/while/body/eval_jaxpr/ppermute | solution.py:12
  350.8 19.8 %collective-permute-start = (bf16[3,22,2048]{2,1,0:T(8,128)(2,1)}, bf16[3,22,2048]{2,1,0:T(8,128)(2,1)}, u32[]{:S(2)}, u32[]{:S(2)}) collective-permute-start(bf16[3,22,2048]{2,1,0:T(8,128)(2,1)} %copy.54), channel_id=1, source_target_pairs={{240,0},{0,16},{16,32},{32,48},{48,64},{64,80},{80,96},{96,112},{1... | collective-permute-start | bytes 811016 | tf_op jit(solution)/shard_map/while/body/eval_jaxpr/ppermute | solution.py:12
  370.6 58.6 %collective-permute-start.8 = (f32[3,22,2048]{2,1,0:T(8,128)}, f32[3,22,2048]{2,1,0:T(8,128)}, u32[]{:S(2)}, u32[]{:S(2)}) collective-permute-start(f32[3,22,2048]{2,1,0:T(8,128)} %get-tuple-element.67), channel_id=1, source_target_pairs={{240,0},{0,16},{16,32},{32,48},{48,64},{64,80},{80,96},{96,112},{1... | collective-permute-start | bytes 1622024 | tf_op jit(solution)/shard_map/ppermute | solution.py:12
  370.7 58.5 %collective-permute-start.10 = (f32[3,22,2048]{2,1,0:T(8,128)}, f32[3,22,2048]{2,1,0:T(8,128)}, u32[]{:S(2)}, u32[]{:S(2)}) collective-permute-start(f32[3,22,2048]{2,1,0:T(8,128)} %get-tuple-element.68), channel_id=1, source_target_pairs={{16,0},{32,16},{48,32},{64,48},{80,64},{96,80},{112,96},{128,112},... | collective-permute-start | bytes 1622024 | tf_op jit(solution)/shard_map/ppermute | solution.py:12
  418.1 173.5 %all-to-all-start.1 = ((bf16[2,16,20,2048]{3,0,2,1:T(2,128)(2,1)}), bf16[2,16,20,2048]{3,0,2,1:T(2,128)(2,1)}, u32[]{:S(2)}, u32[]{:S(2)}) async-start(bf16[2,16,20,2048]{3,0,2,1:T(2,128)(2,1)} %copy.31), calls=%async_computation.1 | async-start | bytes 5242880 | tf_op jit(solution)/shard_map/all_to_all | solution.py:88
  427.4 154.9 %reduce-scatter.2.cloned.1.call-start = ((), (), s32[]{:S(2)}) async-start(), calls=%async_computation.3 | async-start | bytes 1253376 | tf_op jit(solution)/shard_map/reduce_scatter | solution.py:157
  (97 other events, 1097.2 us)
Sparse Core Ops, SparseCore 0:
  441.7 140.5 reduce-scatter.1
